TPU v7x, 256 devices: a whole 4x4x8 slice. The times are simulated.
256 devices in a mesh: resp: 32 (over y, x, core), head: 8 (over z).
Axes of the slice: x: 4, y: 4, z: 8, core: 2. Of those that a mesh axis runs over, the one named last changes fastest.
Arguments:
- queries: bfloat16 [32, 512, 8192], P('resp', None, 'head'), may hold values from -18 to 18
- key_states: bfloat16 [32, 512, 1024], P('resp', None, 'head'), may hold values from -6 to 6
- value_states: bfloat16 [32, 512, 1024], P('resp', None, 'head'), may hold values from -30 to 30
- partners: int32 [32, 3], P('resp'), may hold values from 0 to 31, as said below
- counts: int32 [32], P('resp'), may hold values from 1 to 3, as said below
- norm_gain: float32 [8192], P('head'), may hold values from 0.25 to 1.75
- out_grad: bfloat16 [32, 512, 8192], P('resp', None, 'head'), may hold values from -6 to 6
Outputs:
- normed_out: bfloat16 [32, 512, 8192], P('resp', None, 'head')
- query_grads: bfloat16 [32, 512, 8192], P('resp', None, 'head')
- key_grads: bfloat16 [32, 512, 1024], P('resp', None, 'head')
- value_grads: bfloat16 [32, 512, 1024], P('resp', None, 'head')
Inputs may be any that keep to these rules, and one draw needn't show every extreme that they name: Row r lists 3 different partners, all in the aligned block of 8 responses that holds r, none equal to r; the first counts[r] of them are live, the rest unused. Live partnership is symmetric: b is a live partner of a exactly when a is a live partner of b. `counts`: some response has 3 live partners.
All inputs are finite; a program needn't handle non-finite values.
Results may differ from a plain program's by a relative error of at most 0.015.
Values may be sent and summed in bfloat16 or wider, within the bound.
No kernel may reach another device: no remote copies, remote signals or barrier semaphores. Data moves between devices by JAX's collectives and lax.ppermute only.
A program may use at most 64 MiB of HBM per device.

v0:
```python
import jax
import jax.numpy as jnp
from jax import lax
from jax.sharding import PartitionSpec as P

HD = 128
D = 8192
GROUP = 8
EPSILON = 1e-05
NEG_FLOOR = -1e30


def add_row(buffer, addend, row_index):
    current = lax.dynamic_index_in_dim(buffer, row_index, 0, keepdims=False)
    return lax.dynamic_update_index_in_dim(buffer, current + addend, row_index, 0)


def body(queries, key_states, value_states, partners, counts, norm_gain, out_grad):
    my_index = lax.axis_index("resp")
    seq_len = queries.shape[1]
    kv_cols = key_states.shape[2]
    kv_heads = kv_cols // HD
    per_group = queries.shape[2] // kv_cols
    resp_count = lax.axis_size("resp")

    def by_distance(block):
        rows = [block]
        for distance in range(1, GROUP):
            route = [(low, low ^ distance) for low in range(resp_count)]
            rows.append(lax.ppermute(block, "resp", route))
        return jnp.concatenate(rows, 0)

    cluster_key_rows = by_distance(key_states)
    group_values = by_distance(value_states)
    query_heads = queries[0].reshape(seq_len, kv_heads, per_group, HD)
    score_scale = HD ** (-0.5)
    mate_rows = jnp.bitwise_xor(partners[0], my_index)
    live_count = counts[0]

    def partner_block_tile(slot_index):
        mate_row = mate_rows[slot_index]
        mate_keys = lax.dynamic_index_in_dim(cluster_key_rows, mate_row, 0, keepdims=False).reshape(
            seq_len, kv_heads, HD
        )
        mate_values = lax.dynamic_index_in_dim(group_values, mate_row, 0, keepdims=False).reshape(
            seq_len, kv_heads, HD
        )
        return (mate_keys, mate_values)

    def score_block(mate_keys):
        return (
            jnp.einsum("qhgd,khd->qhgk", query_heads, mate_keys, preferred_element_type=jnp.float32)
            * score_scale
        )

    def forward_step(slot_index, running):
        running_max, denominator, weighted = running
        mate_keys, mate_values = partner_block_tile(slot_index)
        scores = score_block(mate_keys)
        new_max = jnp.maximum(running_max, jnp.max(scores, -1))
        rescale = jnp.exp(running_max - new_max)
        weights = jnp.exp(scores - new_max[..., None])
        denominator = denominator * rescale + jnp.sum(weights, -1)
        weighted = weighted * rescale[..., None] + jnp.einsum(
            "qhgk,khd->qhgd",
            weights.astype(jnp.bfloat16),
            mate_values,
            preferred_element_type=jnp.float32,
        )
        return (new_max, denominator, weighted)

    stat_shape = (seq_len, kv_heads, per_group)
    start_state = (
        jnp.full(stat_shape, NEG_FLOOR, jnp.float32),
        jnp.zeros(stat_shape, jnp.float32),
        jnp.zeros(stat_shape + (HD,), jnp.float32),
    )
    running_max, denominator, weighted = lax.fori_loop(0, live_count, forward_step, start_state)
    attention = (weighted / denominator[..., None]).astype(jnp.bfloat16)
    log_total = running_max + jnp.log(denominator)
    attention_flat = attention.reshape(seq_len, -1).astype(jnp.float32)
    square_sums = lax.psum(jnp.sum(attention_flat * attention_flat, -1), "head")
    inverse_rms = lax.rsqrt(square_sums / D + EPSILON)
    normed_out = (attention_flat * inverse_rms[:, None] * norm_gain).astype(jnp.bfloat16)[None]
    scaled_grad = out_grad[0].astype(jnp.float32) * norm_gain
    dot_sums = lax.psum(jnp.sum(attention_flat * scaled_grad, -1), "head")
    attention_grad = (
        inverse_rms[:, None] * scaled_grad
        - attention_flat * (inverse_rms**3 * dot_sums / D)[:, None]
    )
    attention_grad = attention_grad.astype(jnp.bfloat16).reshape(seq_len, kv_heads, per_group, HD)
    row_delta = jnp.sum(attention_grad.astype(jnp.float32) * attention.astype(jnp.float32), -1)

    def backward_step(slot_index, running):
        query_grad, key_buffer, value_storage = running
        mate_keys, mate_values = partner_block_tile(slot_index)
        back_probs = jnp.exp(score_block(mate_keys) - log_total[..., None])
        value_term = jnp.einsum(
            "qhgk,qhgd->khd",
            back_probs.astype(jnp.bfloat16),
            attention_grad,
            preferred_element_type=jnp.float32,
        )
        prob_grad = jnp.einsum(
            "qhgd,khd->qhgk", attention_grad, mate_values, preferred_element_type=jnp.float32
        )
        score_grad = (back_probs * (prob_grad - row_delta[..., None])).astype(jnp.bfloat16)
        query_grad = query_grad + score_scale * jnp.einsum(
            "qhgk,khd->qhgd", score_grad, mate_keys, preferred_element_type=jnp.float32
        )
        key_term = score_scale * jnp.einsum(
            "qhgk,qhgd->khd", score_grad, query_heads, preferred_element_type=jnp.float32
        )
        mate_row = mate_rows[slot_index]
        key_buffer = add_row(key_buffer, key_term.reshape(seq_len, kv_cols), mate_row)
        value_storage = add_row(value_storage, value_term.reshape(seq_len, kv_cols), mate_row)
        return (query_grad, key_buffer, value_storage)

    zero_buffer = jnp.zeros((GROUP, seq_len, kv_cols), jnp.float32)
    query_grad, key_buffer, value_storage = lax.fori_loop(
        0,
        live_count,
        backward_step,
        (jnp.zeros(stat_shape + (HD,), jnp.float32), zero_buffer, zero_buffer),
    )
    query_grads = query_grad.reshape(seq_len, -1).astype(jnp.bfloat16)[None]

    def to_owners(buffer):
        total = jnp.zeros(buffer.shape[1:], jnp.float32)
        for distance in range(1, GROUP):
            route = [(low, low ^ distance) for low in range(resp_count)]
            sent = buffer[distance].astype(jnp.bfloat16)
            total = total + lax.ppermute(sent, "resp", route).astype(jnp.float32)
        return total[None]

    key_total = to_owners(key_buffer)
    value_total = to_owners(value_storage)
    return (
        normed_out,
        query_grads,
        key_total.astype(jnp.bfloat16),
        value_total.astype(jnp.bfloat16),
    )


def solution(mesh):
    placed = (
        P("resp", None, "head"),
        P("resp", None, "head"),
        P("resp", None, "head"),
        P("resp", None),
        P("resp"),
        P("head"),
        P("resp", None, "head"),
    )
    return jax.shard_map(
        body,
        mesh=mesh,
        in_specs=placed,
        out_specs=(
            P("resp", None, "head"),
            P("resp", None, "head"),
            P("resp", None, "head"),
            P("resp", None, "head"),
        ),
        check_vma=False,
    )
```

profile of v0, /device:TPU:25, one launch (start us, length us, event | category | flops | bytes accessed | tf_op | source)
XLA Modules:
  0.0 200.0 jit_solution(2755921004239567861)
XLA Ops:
  0.6 2.6 %collective-permute-start.5 = (bf16[1,512,128]{2,1,0:T(8,128)(2,1)}, bf16[1,512,128]{2,1,0:T(8,128)(2,1)S(1)}, u32[]{:S(2)}, u32[]{:S(2)}) collective-permute-start(bf16[1,512,128]{2,1,0:T(8,128)(2,1)} %param.12), channel_id=1, source_target_pairs={{0,48},{8,56},{16,32},{24,40},{32,16},{40,24},{48,0},{56,8},{64,11... | collective-permute-start | bytes 393224 | tf_op jit(solution)/shard_map/ppermute | solution.py:30
  4.6 2.5 %collective-permute-start.3 = (bf16[1,512,128]{2,1,0:T(8,128)(2,1)}, bf16[1,512,128]{2,1,0:T(8,128)(2,1)}, u32[]{:S(2)}, u32[]{:S(2)}) collective-permute-start(bf16[1,512,128]{2,1,0:T(8,128)(2,1)} %param.12), channel_id=1, source_target_pairs={{0,32},{8,40},{16,48},{24,56},{32,0},{40,8},{48,16},{56,24},{64,96... | collective-permute-start | bytes 393224 | tf_op jit(solution)/shard_map/ppermute | solution.py:30
  10.2 2.3 %copy.25 = bf16[1,512,1024]{1,2,0:T(8,128)(2,1)} copy(bf16[1,512,1024]{2,1,0:T(8,128)(2,1)} %param.17) | data formatting | bytes 2097152 | tf_op args[6]
  20.4 2.9 %collective-permute-start.11 = (bf16[1,512,128]{2,1,0:T(8,128)(2,1)S(1)}, bf16[1,512,128]{2,1,0:T(8,128)(2,1)S(1)}, u32[]{:S(2)}, u32[]{:S(2)}) collective-permute-start(bf16[1,512,128]{2,1,0:T(8,128)(2,1)S(1)} %copy-done.10), channel_id=1, source_target_pairs={{0,40},{8,32},{16,56},{24,48},{32,8},{40,0},{48,24},{56,16},{64,10... | collective-permute-start | bytes 393224 | tf_op jit(solution)/shard_map/ppermute | solution.py:30
  29.1 3.9 %collective-permute-done.8 = bf16[1,512,128]{2,1,0:T(8,128)(2,1)S(1)} collective-permute-done((bf16[1,512,128]{2,1,0:T(8,128)(2,1)S(1)}, bf16[1,512,128]{2,1,0:T(8,128)(2,1)S(1)}, u32[]{:S(2)}, u32[]{:S(2)}) %collective-permute-start.8) | collective-permute-done | bytes 131104 | tf_op jit(solution)/shard_map/ppermute | solution.py:30
  33.0 2.3 %collective-permute-start.13 = (bf16[1,512,128]{2,1,0:T(8,128)(2,1)S(1)}, bf16[1,512,128]{2,1,0:T(8,128)(2,1)S(1)}, u32[]{:S(2)}, u32[]{:S(2)}) collective-permute-start(bf16[1,512,128]{2,1,0:T(8,128)(2,1)S(1)} %copy-done.10), channel_id=1, source_target_pairs={{0,56},{8,48},{16,40},{24,32},{32,24},{40,16},{48,8},{56,0},{64,12... | collective-permute-start | bytes 393224 | tf_op jit(solution)/shard_map/ppermute | solution.py:30
  40.7 10.9 %while.28 = (s32[]{:T(128)}, f32[512,1,8]{0,2,1:T(8,128)S(1)}, f32[512,1,8]{0,2,1:T(8,128)S(1)}, f32[512,1,8,128]{0,3,2,1:T(8,128)S(1)}, s32[]{:T(128)}, /*index...) while((s32[]{:T(128)}, f32[512,1,8]{0,2,1:T(8,128)S(1)}, ...), condition=%wide.region_3.4_spmd, body=%wide.region_0.3_spmd.sunk | while | flops 1091579904 | bytes 30933212 | solution.py:78
  44.3 2.2 %bitcast_reduce_fusion.2 = (f32[512,8]{0,1:T(8,128)S(1)}, f32[512,512,8]{1,0,2:T(8,128)S(1)}) fusion(bf16[512,1,8,128]{3,0,2,1:T(8,128)(2,1)S(1)} %get-tuple-element.393, bf16[8,512,128]{2,1,0:T(8,128)(2,1)} %get-tuple-element.392, s32[]{:T(128)S(6)} %select_n.27), kind=kOutput, calls=%fused_computation.1.clone.1 | convolution fusion | flops 541061120 | bytes 9584644 | tf_op jit(solution)/shard_map/while/body/qhgd,khd->qhgk/dot_general | solution.py:52
  47.9 3.0 %bitcast_add_fusion.7 = f32[512,1,8,128]{0,3,2,1:T(8,128)S(1)} fusion(f32[512,1,8,128]{0,3,2,1:T(8,128)S(1)} %get-tuple-element.376, f32[512,512,8]{1,0,2:T(8,128)S(1)} %get-tuple-element.346, f32[512,8]{0,1:T(8,128)S(1)} %bitcast.272, f32[512,8]{0,1:T(8,128)S(1)} %get-tuple-element.347, bf16[8,512,128]{2,1,0:T(8,128)(2,1)} %get-tuple-element.394, ...), kind=kOutput, calls=%fused_computation.9.clone.1 | convolution fusion | flops 544210944 | bytes 12746756 | tf_op jit(solution)/shard_map/while/body/qhgk,khd->qhgd/dot_general | solution.py:64
  51.6 2.8 %fusion.60 = (f32[512]{0:T(512)S(1)}, f32[512]{0:T(512)S(1)}, bf16[512,1,8,128]{0,3,2,1:T(8,128)(2,1)}) fusion(bf16[512,1,8,128]{0,3,2,1:T(8,128)(2,1)} %bitcast.273, f32[8,128]{1,0:T(8,128)S(1)} %bitcast.281, f32[512,1,8,128]{0,3,2,1:T(8,128)S(1)} %get-tuple-element.119, f32[512,8]{0,1:T(8,128)S(1)} %bitcast.278), kind=kLoop, calls=%fused_computation.61 | loop fusion | flops 4717568 | bytes 4218880 | tf_op jit(solution)/shard_map/reduce_sum | solution.py:86
  54.4 16.4 %all-reduce = (f32[512]{0:T(512)S(1)}, f32[512]{0:T(512)S(1)}) all-reduce(f32[512]{0:T(512)S(1)} %get-tuple-element.156, f32[512]{0:T(512)S(1)} %get-tuple-element.155), channel_id=1, replica_groups=mesh['resp'=32,'head'=8] {'head'}, use_global_device_ids=true, to_apply=%region_5.6 | all-reduce | flops 1024 | bytes 8192 | tf_op jit(solution)/shard_map/psum | solution.py:82
  82.0 19.0 %while.29 = (s32[]{:T(128)}, f32[512,1,8,128]{0,3,2,1:T(8,128)}, f32[8,512,128]{2,1,0:T(8,128)}, f32[8,512,128]{2,1,0:T(8,128)}, s32[]{:T(128)}, /*index=5*/s32[...) while((s32[]{:T(128)}, f32[512,1,8,128]{0,3,2,1:T(8,128)}, ...), condition=%wide.region_10.11_spmd, body=%wide.region_9.10_spmd.sunk | while | flops 2702376960 | bytes 64405816 | solution.py:120
  85.4 2.2 %fusion.101 = f32[512,512,8]{1,0,2:T(8,128)S(1)} fusion(bf16[512,1,8,128]{3,0,2,1:T(8,128)(2,1)S(1)} %get-tuple-element.438, bf16[8,512,128]{2,1,0:T(8,128)(2,1)} %get-tuple-element.437, s32[]{:T(128)S(6)} %select_n.29), kind=kOutput, calls=%fused_computation.44.clone.1 | convolution fusion | flops 536870912 | bytes 9568260 | tf_op jit(solution)/shard_map/while/body/qhgd,khd->qhgk/dot_general | solution.py:52
  87.6 3.3 %fusion.104 = f32[8,512,128]{2,1,0:T(8,128)} fusion(f32[8,512,128]{2,1,0:T(8,128)} %get-tuple-element.418, s32[]{:T(128)S(6)} %select_n.29, f32[512,512,8]{1,0,2:T(8,128)S(1)} %fusion.101, f32[512,8]{0,1:T(8,128)S(1)} %bitcast.274, bf16[512,1,8,128]{3,0,2,1:T(8,128)(2,1)S(1)} %get-tuple-element.441), kind=kOutput, calls=%fused_computation.38.clone.1 | convolution fusion | flops 543227904 | bytes 9977860 | tf_op jit(solution)/shard_map/while/body/qhgk,qhgd->khd/dot_general | solution.py:98
  90.9 3.1 %fusion.102 = bf16[512,8,512]{0,2,1:T(8,128)(2,1)S(1)} fusion(f32[512,512,8]{1,0,2:T(8,128)S(1)} %fusion.101, f32[512,8]{0,1:T(8,128)S(1)} %bitcast.280, f32[512,8]{0,1:T(8,128)S(1)} %bitcast.275, bf16[512,1,8,128]{3,0,2,1:T(8,128)(2,1)S(1)} %get-tuple-element.441, bf16[8,512,128]{2,1,0:T(8,128)(2,1)} %get-tuple-element.440, s32[]{:T(128)S(6)} %select_n.29), kind=kOutput, calls=%fused_computation.30.clone.1 | convolution fusion | flops 547356672 | bytes 13795332 | tf_op jit(solution)/shard_map/while/body/qhgd,khd->qhgk/dot_general | solution.py:104
  94.0 3.1 %fusion.103 = f32[8,512,128]{2,1,0:T(8,128)} fusion(f32[8,512,128]{2,1,0:T(8,128)} %get-tuple-element.417, s32[]{:T(128)S(6)} %select_n.29, bf16[512,8,512]{0,2,1:T(8,128)(2,1)S(1)} %fusion.102, bf16[512,1,8,128]{3,0,2,1:T(8,128)(2,1)S(1)} %get-tuple-element.438), kind=kOutput, calls=%fused_computation.40.clone.1 | convolution fusion | flops 537001984 | bytes 5767172 | tf_op jit(solution)/shard_map/while/body/qhgk,qhgd->khd/dot_general | solution.py:111
  103.0 32.4 %collective-permute-start.21 = (bf16[512,128]{1,0:T(8,128)(2,1)S(1)}, bf16[512,128]{1,0:T(8,128)(2,1)S(1)}, u32[]{:S(2)}, u32[]{:S(2)}) collective-permute-start(bf16[512,128]{1,0:T(8,128)(2,1)S(1)} %get-tuple-element.206), channel_id=1, source_target_pairs={{0,8},{8,0},{16,24},{24,16},{32,40},{40,32},{48,56},{56,48},{64,72... | collective-permute-start | bytes 393224 | tf_op jit(solution)/shard_map/ppermute | solution.py:133
  135.4 29.5 %collective-permute-start.27 = (bf16[512,128]{1,0:T(8,128)(2,1)S(1)}, bf16[512,128]{1,0:T(8,128)(2,1)S(1)}, u32[]{:S(2)}, u32[]{:S(2)}) collective-permute-start(bf16[512,128]{1,0:T(8,128)(2,1)S(1)} %get-tuple-element.207), channel_id=1, source_target_pairs={{0,56},{8,48},{16,40},{24,32},{32,24},{40,16},{48,8},{56,0},{64,12... | collective-permute-start | bytes 393224 | tf_op jit(solution)/shard_map/ppermute | solution.py:133
  165.0 3.3 %collective-permute-start.24 = (bf16[512,128]{1,0:T(8,128)(2,1)S(1)}, bf16[512,128]{1,0:T(8,128)(2,1)S(1)}, u32[]{:S(2)}, u32[]{:S(2)}) collective-permute-start(bf16[512,128]{1,0:T(8,128)(2,1)S(1)} %get-tuple-element.210), channel_id=1, source_target_pairs={{0,32},{8,40},{16,48},{24,56},{32,0},{40,8},{48,16},{56,24},{64,96... | collective-permute-start | bytes 393224 | tf_op jit(solution)/shard_map/ppermute | solution.py:133
  170.3 6.5 %collective-permute-done.26 = bf16[512,128]{1,0:T(8,128)(2,1)S(1)} collective-permute-done((bf16[512,128]{1,0:T(8,128)(2,1)S(1)}, bf16[512,128]{1,0:T(8,128)(2,1)S(1)}, u32[]{:S(2)}, u32[]{:S(2)}) %collective-permute-start.26) | collective-permute-done | bytes 131104 | tf_op jit(solution)/shard_map/ppermute | solution.py:133
  177.8 2.5 %collective-permute-start.20 = (bf16[512,128]{1,0:T(8,128)(2,1)S(1)}, bf16[512,128]{1,0:T(8,128)(2,1)S(1)}, u32[]{:S(2)}, u32[]{:S(2)}) collective-permute-start(bf16[512,128]{1,0:T(8,128)(2,1)S(1)} %get-tuple-element.214), channel_id=1, source_target_pairs={{0,56},{8,48},{16,40},{24,32},{32,24},{40,16},{48,8},{56,0},{64,12... | collective-permute-start | bytes 393224 | tf_op jit(solution)/shard_map/ppermute | solution.py:133
  183.2 3.5 %collective-permute-start.17 = (bf16[512,128]{1,0:T(8,128)(2,1)S(1)}, bf16[512,128]{1,0:T(8,128)(2,1)S(1)}, u32[]{:S(2)}, u32[]{:S(2)}) collective-permute-start(bf16[512,128]{1,0:T(8,128)(2,1)S(1)} %get-tuple-element.217), channel_id=1, source_target_pairs={{0,32},{8,40},{16,48},{24,56},{32,0},{40,8},{48,16},{56,24},{64,96... | collective-permute-start | bytes 393224 | tf_op jit(solution)/shard_map/ppermute | solution.py:133
  188.9 5.5 %collective-permute-done.19 = bf16[512,128]{1,0:T(8,128)(2,1)S(1)} collective-permute-done((bf16[512,128]{1,0:T(8,128)(2,1)S(1)}, bf16[512,128]{1,0:T(8,128)(2,1)S(1)}, u32[]{:S(2)}, u32[]{:S(2)}) %collective-permute-start.19) | collective-permute-done | bytes 131104 | tf_op jit(solution)/shard_map/ppermute | solution.py:133
  196.4 2.8 %collective-permute-done.15 = bf16[512,128]{1,0:T(8,128)(2,1)S(1)} collective-permute-done((bf16[512,128]{1,0:T(8,128)(2,1)S(1)}, bf16[512,128]{1,0:T(8,128)(2,1)S(1)}, u32[]{:S(2)}, u32[]{:S(2)}) %collective-permute-start.15) | collective-permute-done | bytes 131104 | tf_op jit(solution)/shard_map/ppermute | solution.py:133
  (114 shorter events, 53.7 us)
Async XLA Ops:
  0.6 25.4 %collective-permute-start.5 = (bf16[1,512,128]{2,1,0:T(8,128)(2,1)}, bf16[1,512,128]{2,1,0:T(8,128)(2,1)S(1)}, u32[]{:S(2)}, u32[]{:S(2)}) collective-permute-start(bf16[1,512,128]{2,1,0:T(8,128)(2,1)} %param.12), channel_id=1, source_target_pairs={{0,48},{8,56},{16,32},{24,40},{32,16},{40,24},{48,0},{56,8},{64,11... | collective-permute-start | bytes 393224 | tf_op jit(solution)/shard_map/ppermute | solution.py:30
  3.2 21.0 %collective-permute-start.4 = (bf16[1,512,128]{2,1,0:T(8,128)(2,1)}, bf16[1,512,128]{2,1,0:T(8,128)(2,1)}, u32[]{:S(2)}, u32[]{:S(2)}) collective-permute-start(bf16[1,512,128]{2,1,0:T(8,128)(2,1)} %param.12), channel_id=1, source_target_pairs={{0,40},{8,32},{16,56},{24,48},{32,8},{40,0},{48,24},{56,16},{64,10... | collective-permute-start | bytes 393224 | tf_op jit(solution)/shard_map/ppermute | solution.py:30
  4.6 15.8 %collective-permute-start.3 = (bf16[1,512,128]{2,1,0:T(8,128)(2,1)}, bf16[1,512,128]{2,1,0:T(8,128)(2,1)}, u32[]{:S(2)}, u32[]{:S(2)}) collective-permute-start(bf16[1,512,128]{2,1,0:T(8,128)(2,1)} %param.12), channel_id=1, source_target_pairs={{0,32},{8,40},{16,48},{24,56},{32,0},{40,8},{48,16},{56,24},{64,96... | collective-permute-start | bytes 393224 | tf_op jit(solution)/shard_map/ppermute | solution.py:30
  7.0 9.5 %collective-permute-start.1 = (bf16[1,512,128]{2,1,0:T(8,128)(2,1)}, bf16[1,512,128]{2,1,0:T(8,128)(2,1)}, u32[]{:S(2)}, u32[]{:S(2)}) collective-permute-start(bf16[1,512,128]{2,1,0:T(8,128)(2,1)} %param.12), channel_id=1, source_target_pairs={{0,16},{8,24},{16,0},{24,8},{32,48},{40,56},{48,32},{56,40},{64,80... | collective-permute-start | bytes 393224 | tf_op jit(solution)/shard_map/ppermute | solution.py:30
  16.6 9.6 %collective-permute-start.6 = (bf16[1,512,128]{2,1,0:T(8,128)(2,1)S(1)}, bf16[1,512,128]{2,1,0:T(8,128)(2,1)S(1)}, u32[]{:S(2)}, u32[]{:S(2)}) collective-permute-start(bf16[1,512,128]{2,1,0:T(8,128)(2,1)S(1)} %copy-done.9), channel_id=1, source_target_pairs={{0,56},{8,48},{16,40},{24,32},{32,24},{40,16},{48,8},{56,0},{64,12... | collective-permute-start | bytes 393224 | tf_op jit(solution)/shard_map/ppermute | solution.py:30
  19.4 18.6 %collective-permute-start.12 = (bf16[1,512,128]{2,1,0:T(8,128)(2,1)S(1)}, bf16[1,512,128]{2,1,0:T(8,128)(2,1)S(1)}, u32[]{:S(2)}, u32[]{:S(2)}) collective-permute-start(bf16[1,512,128]{2,1,0:T(8,128)(2,1)S(1)} %copy-done.10), channel_id=1, source_target_pairs={{0,48},{8,56},{16,32},{24,40},{32,16},{40,24},{48,0},{56,8},{64,11... | collective-permute-start | bytes 393224 | tf_op jit(solution)/shard_map/ppermute | solution.py:30
  20.4 16.9 %collective-permute-start.11 = (bf16[1,512,128]{2,1,0:T(8,128)(2,1)S(1)}, bf16[1,512,128]{2,1,0:T(8,128)(2,1)S(1)}, u32[]{:S(2)}, u32[]{:S(2)}) collective-permute-start(bf16[1,512,128]{2,1,0:T(8,128)(2,1)S(1)} %copy-done.10), channel_id=1, source_target_pairs={{0,40},{8,32},{16,56},{24,48},{32,8},{40,0},{48,24},{56,16},{64,10... | collective-permute-start | bytes 393224 | tf_op jit(solution)/shard_map/ppermute | solution.py:30
  24.3 12.4 %collective-permute-start.10 = (bf16[1,512,128]{2,1,0:T(8,128)(2,1)S(1)}, bf16[1,512,128]{2,1,0:T(8,128)(2,1)S(1)}, u32[]{:S(2)}, u32[]{:S(2)}) collective-permute-start(bf16[1,512,128]{2,1,0:T(8,128)(2,1)S(1)} %copy-done.10), channel_id=1, source_target_pairs={{0,32},{8,40},{16,48},{24,56},{32,0},{40,8},{48,16},{56,24},{64,96... | collective-permute-start | bytes 393224 | tf_op jit(solution)/shard_map/ppermute | solution.py:30
  26.2 6.8 %collective-permute-start.8 = (bf16[1,512,128]{2,1,0:T(8,128)(2,1)S(1)}, bf16[1,512,128]{2,1,0:T(8,128)(2,1)S(1)}, u32[]{:S(2)}, u32[]{:S(2)}) collective-permute-start(bf16[1,512,128]{2,1,0:T(8,128)(2,1)S(1)} %copy-done.10), channel_id=1, source_target_pairs={{0,16},{8,24},{16,0},{24,8},{32,48},{40,56},{48,32},{56,40},{64,80... | collective-permute-start | bytes 393224 | tf_op jit(solution)/shard_map/ppermute | solution.py:30
  27.4 8.5 %collective-permute-start.9 = (bf16[1,512,128]{2,1,0:T(8,128)(2,1)S(1)}, bf16[1,512,128]{2,1,0:T(8,128)(2,1)S(1)}, u32[]{:S(2)}, u32[]{:S(2)}) collective-permute-start(bf16[1,512,128]{2,1,0:T(8,128)(2,1)S(1)} %copy-done.10), channel_id=1, source_target_pairs={{0,24},{8,16},{16,8},{24,0},{32,56},{40,48},{48,40},{56,32},{64,88... | collective-permute-start | bytes 393224 | tf_op jit(solution)/shard_map/ppermute | solution.py:30
  103.0 65.5 %collective-permute-start.21 = (bf16[512,128]{1,0:T(8,128)(2,1)S(1)}, bf16[512,128]{1,0:T(8,128)(2,1)S(1)}, u32[]{:S(2)}, u32[]{:S(2)}) collective-permute-start(bf16[512,128]{1,0:T(8,128)(2,1)S(1)} %get-tuple-element.206), channel_id=1, source_target_pairs={{0,8},{8,0},{16,24},{24,16},{32,40},{40,32},{48,56},{56,48},{64,72... | collective-permute-start | bytes 393224 | tf_op jit(solution)/shard_map/ppermute | solution.py:133
  135.4 34.0 %collective-permute-start.27 = (bf16[512,128]{1,0:T(8,128)(2,1)S(1)}, bf16[512,128]{1,0:T(8,128)(2,1)S(1)}, u32[]{:S(2)}, u32[]{:S(2)}) collective-permute-start(bf16[512,128]{1,0:T(8,128)(2,1)S(1)} %get-tuple-element.207), channel_id=1, source_target_pairs={{0,56},{8,48},{16,40},{24,32},{32,24},{40,16},{48,8},{56,0},{64,12... | collective-permute-start | bytes 393224 | tf_op jit(solution)/shard_map/ppermute | solution.py:133
  164.9 11.9 %collective-permute-start.26 = (bf16[512,128]{1,0:T(8,128)(2,1)S(1)}, bf16[512,128]{1,0:T(8,128)(2,1)S(1)}, u32[]{:S(2)}, u32[]{:S(2)}) collective-permute-start(bf16[512,128]{1,0:T(8,128)(2,1)S(1)} %get-tuple-element.208), channel_id=1, source_target_pairs={{0,48},{8,56},{16,32},{24,40},{32,16},{40,24},{48,0},{56,8},{64,11... | collective-permute-start | bytes 393224 | tf_op jit(solution)/shard_map/ppermute | solution.py:133
  165.0 12.8 %collective-permute-start.25 = (bf16[512,128]{1,0:T(8,128)(2,1)S(1)}, bf16[512,128]{1,0:T(8,128)(2,1)S(1)}, u32[]{:S(2)}, u32[]{:S(2)}) collective-permute-start(bf16[512,128]{1,0:T(8,128)(2,1)S(1)} %get-tuple-element.209), channel_id=1, source_target_pairs={{0,40},{8,32},{16,56},{24,48},{32,8},{40,0},{48,24},{56,16},{64,10... | collective-permute-start | bytes 393224 | tf_op jit(solution)/shard_map/ppermute | solution.py:133
  165.0 18.1 %collective-permute-start.24 = (bf16[512,128]{1,0:T(8,128)(2,1)S(1)}, bf16[512,128]{1,0:T(8,128)(2,1)S(1)}, u32[]{:S(2)}, u32[]{:S(2)}) collective-permute-start(bf16[512,128]{1,0:T(8,128)(2,1)S(1)} %get-tuple-element.210), channel_id=1, source_target_pairs={{0,32},{8,40},{16,48},{24,56},{32,0},{40,8},{48,16},{56,24},{64,96... | collective-permute-start | bytes 393224 | tf_op jit(solution)/shard_map/ppermute | solution.py:133
  168.5 14.6 %collective-permute-start.23 = (bf16[512,128]{1,0:T(8,128)(2,1)S(1)}, bf16[512,128]{1,0:T(8,128)(2,1)S(1)}, u32[]{:S(2)}, u32[]{:S(2)}) collective-permute-start(bf16[512,128]{1,0:T(8,128)(2,1)S(1)} %get-tuple-element.211), channel_id=1, source_target_pairs={{0,24},{8,16},{16,8},{24,0},{32,56},{40,48},{48,40},{56,32},{64,88... | collective-permute-start | bytes 393224 | tf_op jit(solution)/shard_map/ppermute | solution.py:133
  169.4 13.7 %collective-permute-start.22 = (bf16[512,128]{1,0:T(8,128)(2,1)S(1)}, bf16[512,128]{1,0:T(8,128)(2,1)S(1)}, u32[]{:S(2)}, u32[]{:S(2)}) collective-permute-start(bf16[512,128]{1,0:T(8,128)(2,1)S(1)} %get-tuple-element.212), channel_id=1, source_target_pairs={{0,16},{8,24},{16,0},{24,8},{32,48},{40,56},{48,32},{56,40},{64,80... | collective-permute-start | bytes 393224 | tf_op jit(solution)/shard_map/ppermute | solution.py:133
  176.8 9.9 %collective-permute-start.14 = (bf16[512,128]{1,0:T(8,128)(2,1)S(1)}, bf16[512,128]{1,0:T(8,128)(2,1)S(1)}, u32[]{:S(2)}, u32[]{:S(2)}) collective-permute-start(bf16[512,128]{1,0:T(8,128)(2,1)S(1)} %get-tuple-element.213), channel_id=1, source_target_pairs={{0,8},{8,0},{16,24},{24,16},{32,40},{40,32},{48,56},{56,48},{64,72... | collective-permute-start | bytes 393224 | tf_op jit(solution)/shard_map/ppermute | solution.py:133
  177.8 9.5 %collective-permute-start.20 = (bf16[512,128]{1,0:T(8,128)(2,1)S(1)}, bf16[512,128]{1,0:T(8,128)(2,1)S(1)}, u32[]{:S(2)}, u32[]{:S(2)}) collective-permute-start(bf16[512,128]{1,0:T(8,128)(2,1)S(1)} %get-tuple-element.214), channel_id=1, source_target_pairs={{0,56},{8,48},{16,40},{24,32},{32,24},{40,16},{48,8},{56,0},{64,12... | collective-permute-start | bytes 393224 | tf_op jit(solution)/shard_map/ppermute | solution.py:133
  183.0 11.4 %collective-permute-start.19 = (bf16[512,128]{1,0:T(8,128)(2,1)S(1)}, bf16[512,128]{1,0:T(8,128)(2,1)S(1)}, u32[]{:S(2)}, u32[]{:S(2)}) collective-permute-start(bf16[512,128]{1,0:T(8,128)(2,1)S(1)} %get-tuple-element.215), channel_id=1, source_target_pairs={{0,48},{8,56},{16,32},{24,40},{32,16},{40,24},{48,0},{56,8},{64,11... | collective-permute-start | bytes 393224 | tf_op jit(solution)/shard_map/ppermute | solution.py:133
  183.2 11.3 %collective-permute-start.18 = (bf16[512,128]{1,0:T(8,128)(2,1)S(1)}, bf16[512,128]{1,0:T(8,128)(2,1)S(1)}, u32[]{:S(2)}, u32[]{:S(2)}) collective-permute-start(bf16[512,128]{1,0:T(8,128)(2,1)S(1)} %get-tuple-element.216), channel_id=1, source_target_pairs={{0,40},{8,32},{16,56},{24,48},{32,8},{40,0},{48,24},{56,16},{64,10... | collective-permute-start | bytes 393224 | tf_op jit(solution)/shard_map/ppermute | solution.py:133
  183.2 11.3 %collective-permute-start.17 = (bf16[512,128]{1,0:T(8,128)(2,1)S(1)}, bf16[512,128]{1,0:T(8,128)(2,1)S(1)}, u32[]{:S(2)}, u32[]{:S(2)}) collective-permute-start(bf16[512,128]{1,0:T(8,128)(2,1)S(1)} %get-tuple-element.217), channel_id=1, source_target_pairs={{0,32},{8,40},{16,48},{24,56},{32,0},{40,8},{48,16},{56,24},{64,96... | collective-permute-start | bytes 393224 | tf_op jit(solution)/shard_map/ppermute | solution.py:133
  186.7 9.7 %collective-permute-start.16 = (bf16[512,128]{1,0:T(8,128)(2,1)S(1)}, bf16[512,128]{1,0:T(8,128)(2,1)S(1)}, u32[]{:S(2)}, u32[]{:S(2)}) collective-permute-start(bf16[512,128]{1,0:T(8,128)(2,1)S(1)} %get-tuple-element.218), channel_id=1, source_target_pairs={{0,24},{8,16},{16,8},{24,0},{32,56},{40,48},{48,40},{56,32},{64,88... | collective-permute-start | bytes 393224 | tf_op jit(solution)/shard_map/ppermute | solution.py:133
  187.4 11.9 %collective-permute-start.15 = (bf16[512,128]{1,0:T(8,128)(2,1)S(1)}, bf16[512,128]{1,0:T(8,128)(2,1)S(1)}, u32[]{:S(2)}, u32[]{:S(2)}) collective-permute-start(bf16[512,128]{1,0:T(8,128)(2,1)S(1)} %get-tuple-element.219), channel_id=1, source_target_pairs={{0,16},{8,24},{16,0},{24,8},{32,48},{40,56},{48,32},{56,40},{64,80... | collective-permute-start | bytes 393224 | tf_op jit(solution)/shard_map/ppermute | solution.py:133
  (16 other events, 182.0 us)
where the time goes:
time: 201 us; the launch traced here: 200 us
  starting transfers between devices  93.6 us (47%)
  local copies, waits for them, and re-layouts  27.5 us (14%)
  waiting for transfers between devices  23.6 us (12%)
  matrix products  18.7 us (9%)
  blocking collectives  16.4 us (8%)
  other arithmetic  12.1 us (6%)
  loops' own time  7.14 us (4%)
    ppermute x14, starting transfers between devices, to_owners(): total = total + lax.ppermute(sent, 'resp', route).astype(jnp.float32)  75.7 us
    ppermute x14, starting transfers between devices, by_distance(): rows.append(lax.ppermute(block, 'resp', route))  17.9 us
    ppermute x14, waiting for transfers between devices, to_owners(): total = total + lax.ppermute(sent, 'resp', route).astype(jnp.float32)  16.8 us
    psum x1, blocking collectives, body(): square_sums = lax.psum(jnp.sum(attention_flat * attention_flat, -1), 'head')  16.4 us
    unnamed x36, local copies, waits for them, and re-layouts  14 us
    ppermute x14, waiting for transfers between devices, by_distance(): rows.append(lax.ppermute(block, 'resp', route))  6.82 us
    dot_general x2, matrix products, score_block(): jnp.einsum('qhgd,khd->qhgk', query_heads, mate_keys, preferred_element_ty...  4.33 us
  transfers between devices with their start and end apart: 28, of which 8 were waited for; matrix products, arithmetic and copies ran while one was open for 9% of the time, Pallas kernels for 0%

commit v1 on v0

--- a/solution.py
+++ b/solution.py
@@ -1,3 +1,4 @@
+import functools
 import jax
 import jax.numpy as jnp
 from jax import lax
@@ -8,6 +9,13 @@
 GROUP = 8
 EPSILON = 1e-05
 NEG_FLOOR = -1e30
+
+
+def _feed_pipes(base_x, dev_axis):
+    return lax.all_gather(base_x, dev_axis).sum(axis=0)
+
+
+load_panel = functools.partial(_feed_pipes, dev_axis="head")
 
 
 def add_row(buffer, addend, row_index):
@@ -79,7 +87,7 @@
     attention = (weighted / denominator[..., None]).astype(jnp.bfloat16)
     log_total = running_max + jnp.log(denominator)
     attention_flat = attention.reshape(seq_len, -1).astype(jnp.float32)
-    square_sums = lax.psum(jnp.sum(attention_flat * attention_flat, -1), "head")
+    square_sums = load_panel(jnp.sum(attention_flat * attention_flat, -1))
     inverse_rms = lax.rsqrt(square_sums / D + EPSILON)
     normed_out = (attention_flat * inverse_rms[:, None] * norm_gain).astype(jnp.bfloat16)[None]
     scaled_grad = out_grad[0].astype(jnp.float32) * norm_gain

time: 201 us -> 222 us (1.10)
  blocking collectives: 16.4 us -> 32.4 us
  starting transfers between devices: 93.6 us -> 98.2 us
    all_gather x0 -> x1, blocking collectives: none -> 16 us  [_feed_pipes(): return lax.all_gather(base_x, dev_axis).sum(axis=0)]
    ppermute x14, starting transfers between devices: 75.7 us -> 80.3 us  [to_owners(): total = total + lax.ppermute(sent, 'resp', route).astype(jnp.float32)]
  transfers between devices with their start and end apart: 28 -> 28, of which waited for: 8 -> 8; matrix products, arithmetic and copies ran while one was open for 9% -> 8% of each run, Pallas kernels for 0% -> 0%
where the time goes in v1:
time: 222 us; the launch traced here: 221 us
  starting transfers between devices  98.2 us (44%)
  blocking collectives  32.4 us (15%)
  local copies, waits for them, and re-layouts  27.4 us (12%)
  waiting for transfers between devices  23.6 us (11%)
  matrix products  18.7 us (8%)
  other arithmetic  12.2 us (5%)
  loops' own time  7.08 us (3%)
    ppermute x14, starting transfers between devices, to_owners(): total = total + lax.ppermute(sent, 'resp', route).astype(jnp.float32)  80.3 us
    ppermute x14, starting transfers between devices, by_distance(): rows.append(lax.ppermute(block, 'resp', route))  17.9 us
    ppermute x14, waiting for transfers between devices, to_owners(): total = total + lax.ppermute(sent, 'resp', route).astype(jnp.float32)  16.8 us
    psum x1, blocking collectives, body(): dot_sums = lax.psum(jnp.sum(attention_flat * scaled_grad, -1), 'head')  16.4 us
    all_gather x1, blocking collectives, _feed_pipes(): return lax.all_gather(base_x, dev_axis).sum(axis=0)  16 us
    unnamed x36, local copies, waits for them, and re-layouts  14 us
    ppermute x14, waiting for transfers between devices, by_distance(): rows.append(lax.ppermute(block, 'resp', route))  6.83 us
  transfers between devices with their start and end apart: 28, of which 8 were waited for; matrix products, arithmetic and copies ran while one was open for 8% of the time, Pallas kernels for 0%

profile of v1, /device:TPU:25, one launch (start us, length us, event | category | flops | bytes accessed | tf_op | source)
XLA Modules:
  0.0 220.5 jit_solution(10513865416272695256)
XLA Ops:
  0.6 2.6 %collective-permute-start.5 = (bf16[1,512,128]{2,1,0:T(8,128)(2,1)}, bf16[1,512,128]{2,1,0:T(8,128)(2,1)S(1)}, u32[]{:S(2)}, u32[]{:S(2)}) collective-permute-start(bf16[1,512,128]{2,1,0:T(8,128)(2,1)} %param.12), channel_id=1, source_target_pairs={{0,48},{8,56},{16,32},{24,40},{32,16},{40,24},{48,0},{56,8},{64,11... | collective-permute-start | bytes 393224 | tf_op jit(solution)/shard_map/ppermute | solution.py:38
  4.6 2.5 %collective-permute-start.3 = (bf16[1,512,128]{2,1,0:T(8,128)(2,1)}, bf16[1,512,128]{2,1,0:T(8,128)(2,1)}, u32[]{:S(2)}, u32[]{:S(2)}) collective-permute-start(bf16[1,512,128]{2,1,0:T(8,128)(2,1)} %param.12), channel_id=1, source_target_pairs={{0,32},{8,40},{16,48},{24,56},{32,0},{40,8},{48,16},{56,24},{64,96... | collective-permute-start | bytes 393224 | tf_op jit(solution)/shard_map/ppermute | solution.py:38
  10.2 2.3 %copy.36 = bf16[1,512,1024]{1,2,0:T(8,128)(2,1)} copy(bf16[1,512,1024]{2,1,0:T(8,128)(2,1)} %param.17) | data formatting | bytes 2097152 | tf_op args[6]
  20.4 2.9 %collective-permute-start.11 = (bf16[1,512,128]{2,1,0:T(8,128)(2,1)S(1)}, bf16[1,512,128]{2,1,0:T(8,128)(2,1)S(1)}, u32[]{:S(2)}, u32[]{:S(2)}) collective-permute-start(bf16[1,512,128]{2,1,0:T(8,128)(2,1)S(1)} %copy-done.10), channel_id=1, source_target_pairs={{0,40},{8,32},{16,56},{24,48},{32,8},{40,0},{48,24},{56,16},{64,10... | collective-permute-start | bytes 393224 | tf_op jit(solution)/shard_map/ppermute | solution.py:38
  29.1 3.9 %collective-permute-done.8 = bf16[1,512,128]{2,1,0:T(8,128)(2,1)S(1)} collective-permute-done((bf16[1,512,128]{2,1,0:T(8,128)(2,1)S(1)}, bf16[1,512,128]{2,1,0:T(8,128)(2,1)S(1)}, u32[]{:S(2)}, u32[]{:S(2)}) %collective-permute-start.8) | collective-permute-done | bytes 131104 | tf_op jit(solution)/shard_map/ppermute | solution.py:38
  33.0 2.3 %collective-permute-start.13 = (bf16[1,512,128]{2,1,0:T(8,128)(2,1)S(1)}, bf16[1,512,128]{2,1,0:T(8,128)(2,1)S(1)}, u32[]{:S(2)}, u32[]{:S(2)}) collective-permute-start(bf16[1,512,128]{2,1,0:T(8,128)(2,1)S(1)} %copy-done.10), channel_id=1, source_target_pairs={{0,56},{8,48},{16,40},{24,32},{32,24},{40,16},{48,8},{56,0},{64,12... | collective-permute-start | bytes 393224 | tf_op jit(solution)/shard_map/ppermute | solution.py:38
  40.7 10.8 %while.28 = (s32[]{:T(128)}, f32[512,1,8]{0,2,1:T(8,128)S(1)}, f32[512,1,8]{0,2,1:T(8,128)S(1)}, f32[512,1,8,128]{0,3,2,1:T(8,128)S(1)}, s32[]{:T(128)}, /*index...) while((s32[]{:T(128)}, f32[512,1,8]{0,2,1:T(8,128)S(1)}, ...), condition=%wide.region_3.4_spmd, body=%wide.region_0.3_spmd.sunk | while | flops 1091579904 | bytes 30933212 | solution.py:86
  44.3 2.2 bitcast_reduce_fusion.2
  47.8 3.0 %bitcast_add_fusion.7 = f32[512,1,8,128]{0,3,2,1:T(8,128)S(1)} fusion(f32[512,1,8,128]{0,3,2,1:T(8,128)S(1)} %get-tuple-element.395, f32[512,512,8]{1,0,2:T(8,128)S(1)} %get-tuple-element.365, f32[512,8]{0,1:T(8,128)S(1)} %bitcast.273, f32[512,8]{0,1:T(8,128)S(1)} %get-tuple-element.366, bf16[8,512,128]{2,1,0:T(8,128)(2,1)} %get-tuple-element.413, ...), kind=kOutput, calls=%fused_computation.9.clone.1 | convolution fusion | flops 544210944 | bytes 12746756 | tf_op jit(solution)/shard_map/while/body/qhgk,khd->qhgd/dot_general | solution.py:72
  51.6 2.8 %fusion.60 = (f32[512]{0:T(512)S(1)}, f32[512]{0:T(512)S(1)}, bf16[512,1,8,128]{0,3,2,1:T(8,128)(2,1)}) fusion(bf16[512,1,8,128]{0,3,2,1:T(8,128)(2,1)} %bitcast.274, f32[8,128]{1,0:T(8,128)S(1)} %bitcast.282, f32[512,1,8,128]{0,3,2,1:T(8,128)S(1)} %get-tuple-element.119, f32[512,8]{0,1:T(8,128)S(1)} %bitcast.279), kind=kLoop, calls=%fused_computation.61 | loop fusion | flops 4717568 | bytes 4218880 | tf_op jit(solution)/shard_map/reduce_sum | solution.py:94
  54.3 16.4 %psum.7 = f32[512]{0:T(512)S(1)} all-reduce(f32[512]{0:T(512)S(1)} %get-tuple-element.176), channel_id=1, replica_groups=mesh['resp'=32,'head'=8] {'head'}, use_global_device_ids=true, to_apply=%region_7.8 | all-reduce | flops 512 | bytes 4096 | tf_op jit(solution)/shard_map/psum | solution.py:94
  70.7 16.0 %all-gather.1 = f32[8,1,512]{2,1,0:T(1,128)S(1)} all-gather(f32[1,1,512]{2,1,0:T(1,128)S(1)} %bitcast.284), channel_id=2, replica_groups=mesh['resp'=32,'head'=8] {'head'}, dimensions={0}, use_global_device_ids=true | all-gather | bytes 18432 | tf_op jit(solution)/shard_map/all_gather | solution.py:15
  98.0 19.0 %while.29 = (s32[]{:T(128)}, f32[512,1,8,128]{0,3,2,1:T(8,128)}, f32[8,512,128]{2,1,0:T(8,128)}, f32[8,512,128]{2,1,0:T(8,128)}, s32[]{:T(128)}, /*index=5*/s32[...) while((s32[]{:T(128)}, f32[512,1,8,128]{0,3,2,1:T(8,128)}, ...), condition=%wide.region_10.11_spmd, body=%wide.region_9.10_spmd.sunk | while | flops 2702376960 | bytes 64405816 | solution.py:128
  103.6 3.3 %fusion.104 = f32[8,512,128]{2,1,0:T(8,128)} fusion(f32[8,512,128]{2,1,0:T(8,128)} %get-tuple-element.437, s32[]{:T(128)S(6)} %select_n.29, f32[512,512,8]{1,0,2:T(8,128)S(1)} %fusion.101, f32[512,8]{0,1:T(8,128)S(1)} %bitcast.275, bf16[512,1,8,128]{3,0,2,1:T(8,128)(2,1)S(1)} %get-tuple-element.460), kind=kOutput, calls=%fused_computation.38.clone.1 | convolution fusion | flops 543227904 | bytes 9977860 | tf_op jit(solution)/shard_map/while/body/qhgk,qhgd->khd/dot_general | solution.py:106
  106.9 3.1 %fusion.102 = bf16[512,8,512]{0,2,1:T(8,128)(2,1)S(1)} fusion(f32[512,512,8]{1,0,2:T(8,128)S(1)} %fusion.101, f32[512,8]{0,1:T(8,128)S(1)} %bitcast.281, f32[512,8]{0,1:T(8,128)S(1)} %bitcast.276, bf16[512,1,8,128]{3,0,2,1:T(8,128)(2,1)S(1)} %get-tuple-element.460, bf16[8,512,128]{2,1,0:T(8,128)(2,1)} %get-tuple-element.459, s32[]{:T(128)S(6)} %select_n.29), kind=kOutput, calls=%fused_computation.30.clone.1 | convolution fusion | flops 547356672 | bytes 13795332 | tf_op jit(solution)/shard_map/while/body/qhgd,khd->qhgk/dot_general | solution.py:112
  110.0 3.0 %fusion.103 = f32[8,512,128]{2,1,0:T(8,128)} fusion(f32[8,512,128]{2,1,0:T(8,128)} %get-tuple-element.436, s32[]{:T(128)S(6)} %select_n.29, bf16[512,8,512]{0,2,1:T(8,128)(2,1)S(1)} %fusion.102, bf16[512,1,8,128]{3,0,2,1:T(8,128)(2,1)S(1)} %get-tuple-element.457), kind=kOutput, calls=%fused_computation.40.clone.1 | convolution fusion | flops 537001984 | bytes 5767172 | tf_op jit(solution)/shard_map/while/body/qhgk,qhgd->khd/dot_general | solution.py:119
  119.0 37.1 %collective-permute-start.21 = (bf16[512,128]{1,0:T(8,128)(2,1)S(1)}, bf16[512,128]{1,0:T(8,128)(2,1)S(1)}, u32[]{:S(2)}, u32[]{:S(2)}) collective-permute-start(bf16[512,128]{1,0:T(8,128)(2,1)S(1)} %get-tuple-element.225), channel_id=1, source_target_pairs={{0,8},{8,0},{16,24},{24,16},{32,40},{40,32},{48,56},{56,48},{64,72... | collective-permute-start | bytes 393224 | tf_op jit(solution)/shard_map/ppermute | solution.py:141
  156.0 29.4 %collective-permute-start.27 = (bf16[512,128]{1,0:T(8,128)(2,1)S(1)}, bf16[512,128]{1,0:T(8,128)(2,1)S(1)}, u32[]{:S(2)}, u32[]{:S(2)}) collective-permute-start(bf16[512,128]{1,0:T(8,128)(2,1)S(1)} %get-tuple-element.226), channel_id=1, source_target_pairs={{0,56},{8,48},{16,40},{24,32},{32,24},{40,16},{48,8},{56,0},{64,12... | collective-permute-start | bytes 393224 | tf_op jit(solution)/shard_map/ppermute | solution.py:141
  185.5 3.3 %collective-permute-start.24 = (bf16[512,128]{1,0:T(8,128)(2,1)S(1)}, bf16[512,128]{1,0:T(8,128)(2,1)S(1)}, u32[]{:S(2)}, u32[]{:S(2)}) collective-permute-start(bf16[512,128]{1,0:T(8,128)(2,1)S(1)} %get-tuple-element.229), channel_id=1, source_target_pairs={{0,32},{8,40},{16,48},{24,56},{32,0},{40,8},{48,16},{56,24},{64,96... | collective-permute-start | bytes 393224 | tf_op jit(solution)/shard_map/ppermute | solution.py:141
  190.8 6.5 %collective-permute-done.26 = bf16[512,128]{1,0:T(8,128)(2,1)S(1)} collective-permute-done((bf16[512,128]{1,0:T(8,128)(2,1)S(1)}, bf16[512,128]{1,0:T(8,128)(2,1)S(1)}, u32[]{:S(2)}, u32[]{:S(2)}) %collective-permute-start.26) | collective-permute-done | bytes 131104 | tf_op jit(solution)/shard_map/ppermute | solution.py:141
  198.3 2.5 %collective-permute-start.20 = (bf16[512,128]{1,0:T(8,128)(2,1)S(1)}, bf16[512,128]{1,0:T(8,128)(2,1)S(1)}, u32[]{:S(2)}, u32[]{:S(2)}) collective-permute-start(bf16[512,128]{1,0:T(8,128)(2,1)S(1)} %get-tuple-element.233), channel_id=1, source_target_pairs={{0,56},{8,48},{16,40},{24,32},{32,24},{40,16},{48,8},{56,0},{64,12... | collective-permute-start | bytes 393224 | tf_op jit(solution)/shard_map/ppermute | solution.py:141
  203.7 3.5 %collective-permute-start.17 = (bf16[512,128]{1,0:T(8,128)(2,1)S(1)}, bf16[512,128]{1,0:T(8,128)(2,1)S(1)}, u32[]{:S(2)}, u32[]{:S(2)}) collective-permute-start(bf16[512,128]{1,0:T(8,128)(2,1)S(1)} %get-tuple-element.236), channel_id=1, source_target_pairs={{0,32},{8,40},{16,48},{24,56},{32,0},{40,8},{48,16},{56,24},{64,96... | collective-permute-start | bytes 393224 | tf_op jit(solution)/shard_map/ppermute | solution.py:141
  209.5 5.5 %collective-permute-done.19 = bf16[512,128]{1,0:T(8,128)(2,1)S(1)} collective-permute-done((bf16[512,128]{1,0:T(8,128)(2,1)S(1)}, bf16[512,128]{1,0:T(8,128)(2,1)S(1)}, u32[]{:S(2)}, u32[]{:S(2)}) %collective-permute-start.19) | collective-permute-done | bytes 131104 | tf_op jit(solution)/shard_map/ppermute | solution.py:141
  217.0 2.8 %collective-permute-done.15 = bf16[512,128]{1,0:T(8,128)(2,1)S(1)} collective-permute-done((bf16[512,128]{1,0:T(8,128)(2,1)S(1)}, bf16[512,128]{1,0:T(8,128)(2,1)S(1)}, u32[]{:S(2)}, u32[]{:S(2)}) %collective-permute-start.15) | collective-permute-done | bytes 131104 | tf_op jit(solution)/shard_map/ppermute | solution.py:141
  (116 shorter events, 55.8 us)
Async XLA Ops:
  0.6 25.4 %collective-permute-start.5 = (bf16[1,512,128]{2,1,0:T(8,128)(2,1)}, bf16[1,512,128]{2,1,0:T(8,128)(2,1)S(1)}, u32[]{:S(2)}, u32[]{:S(2)}) collective-permute-start(bf16[1,512,128]{2,1,0:T(8,128)(2,1)} %param.12), channel_id=1, source_target_pairs={{0,48},{8,56},{16,32},{24,40},{32,16},{40,24},{48,0},{56,8},{64,11... | collective-permute-start | bytes 393224 | tf_op jit(solution)/shard_map/ppermute | solution.py:38
  3.2 21.0 %collective-permute-start.4 = (bf16[1,512,128]{2,1,0:T(8,128)(2,1)}, bf16[1,512,128]{2,1,0:T(8,128)(2,1)}, u32[]{:S(2)}, u32[]{:S(2)}) collective-permute-start(bf16[1,512,128]{2,1,0:T(8,128)(2,1)} %param.12), channel_id=1, source_target_pairs={{0,40},{8,32},{16,56},{24,48},{32,8},{40,0},{48,24},{56,16},{64,10... | collective-permute-start | bytes 393224 | tf_op jit(solution)/shard_map/ppermute | solution.py:38
  4.6 15.8 %collective-permute-start.3 = (bf16[1,512,128]{2,1,0:T(8,128)(2,1)}, bf16[1,512,128]{2,1,0:T(8,128)(2,1)}, u32[]{:S(2)}, u32[]{:S(2)}) collective-permute-start(bf16[1,512,128]{2,1,0:T(8,128)(2,1)} %param.12), channel_id=1, source_target_pairs={{0,32},{8,40},{16,48},{24,56},{32,0},{40,8},{48,16},{56,24},{64,96... | collective-permute-start | bytes 393224 | tf_op jit(solution)/shard_map/ppermute | solution.py:38
  7.0 9.5 %collective-permute-start.1 = (bf16[1,512,128]{2,1,0:T(8,128)(2,1)}, bf16[1,512,128]{2,1,0:T(8,128)(2,1)}, u32[]{:S(2)}, u32[]{:S(2)}) collective-permute-start(bf16[1,512,128]{2,1,0:T(8,128)(2,1)} %param.12), channel_id=1, source_target_pairs={{0,16},{8,24},{16,0},{24,8},{32,48},{40,56},{48,32},{56,40},{64,80... | collective-permute-start | bytes 393224 | tf_op jit(solution)/shard_map/ppermute | solution.py:38
  16.6 9.6 %collective-permute-start.6 = (bf16[1,512,128]{2,1,0:T(8,128)(2,1)S(1)}, bf16[1,512,128]{2,1,0:T(8,128)(2,1)S(1)}, u32[]{:S(2)}, u32[]{:S(2)}) collective-permute-start(bf16[1,512,128]{2,1,0:T(8,128)(2,1)S(1)} %copy-done.9), channel_id=1, source_target_pairs={{0,56},{8,48},{16,40},{24,32},{32,24},{40,16},{48,8},{56,0},{64,12... | collective-permute-start | bytes 393224 | tf_op jit(solution)/shard_map/ppermute | solution.py:38
  19.4 18.6 %collective-permute-start.12 = (bf16[1,512,128]{2,1,0:T(8,128)(2,1)S(1)}, bf16[1,512,128]{2,1,0:T(8,128)(2,1)S(1)}, u32[]{:S(2)}, u32[]{:S(2)}) collective-permute-start(bf16[1,512,128]{2,1,0:T(8,128)(2,1)S(1)} %copy-done.10), channel_id=1, source_target_pairs={{0,48},{8,56},{16,32},{24,40},{32,16},{40,24},{48,0},{56,8},{64,11... | collective-permute-start | bytes 393224 | tf_op jit(solution)/shard_map/ppermute | solution.py:38
  20.4 16.9 %collective-permute-start.11 = (bf16[1,512,128]{2,1,0:T(8,128)(2,1)S(1)}, bf16[1,512,128]{2,1,0:T(8,128)(2,1)S(1)}, u32[]{:S(2)}, u32[]{:S(2)}) collective-permute-start(bf16[1,512,128]{2,1,0:T(8,128)(2,1)S(1)} %copy-done.10), channel_id=1, source_target_pairs={{0,40},{8,32},{16,56},{24,48},{32,8},{40,0},{48,24},{56,16},{64,10... | collective-permute-start | bytes 393224 | tf_op jit(solution)/shard_map/ppermute | solution.py:38
  24.3 12.4 %collective-permute-start.10 = (bf16[1,512,128]{2,1,0:T(8,128)(2,1)S(1)}, bf16[1,512,128]{2,1,0:T(8,128)(2,1)S(1)}, u32[]{:S(2)}, u32[]{:S(2)}) collective-permute-start(bf16[1,512,128]{2,1,0:T(8,128)(2,1)S(1)} %copy-done.10), channel_id=1, source_target_pairs={{0,32},{8,40},{16,48},{24,56},{32,0},{40,8},{48,16},{56,24},{64,96... | collective-permute-start | bytes 393224 | tf_op jit(solution)/shard_map/ppermute | solution.py:38
  26.2 6.8 %collective-permute-start.8 = (bf16[1,512,128]{2,1,0:T(8,128)(2,1)S(1)}, bf16[1,512,128]{2,1,0:T(8,128)(2,1)S(1)}, u32[]{:S(2)}, u32[]{:S(2)}) collective-permute-start(bf16[1,512,128]{2,1,0:T(8,128)(2,1)S(1)} %copy-done.10), channel_id=1, source_target_pairs={{0,16},{8,24},{16,0},{24,8},{32,48},{40,56},{48,32},{56,40},{64,80... | collective-permute-start | bytes 393224 | tf_op jit(solution)/shard_map/ppermute | solution.py:38
  27.4 8.5 %collective-permute-start.9 = (bf16[1,512,128]{2,1,0:T(8,128)(2,1)S(1)}, bf16[1,512,128]{2,1,0:T(8,128)(2,1)S(1)}, u32[]{:S(2)}, u32[]{:S(2)}) collective-permute-start(bf16[1,512,128]{2,1,0:T(8,128)(2,1)S(1)} %copy-done.10), channel_id=1, source_target_pairs={{0,24},{8,16},{16,8},{24,0},{32,56},{40,48},{48,40},{56,32},{64,88... | collective-permute-start | bytes 393224 | tf_op jit(solution)/shard_map/ppermute | solution.py:38
  119.0 70.1 %collective-permute-start.21 = (bf16[512,128]{1,0:T(8,128)(2,1)S(1)}, bf16[512,128]{1,0:T(8,128)(2,1)S(1)}, u32[]{:S(2)}, u32[]{:S(2)}) collective-permute-start(bf16[512,128]{1,0:T(8,128)(2,1)S(1)} %get-tuple-element.225), channel_id=1, source_target_pairs={{0,8},{8,0},{16,24},{24,16},{32,40},{40,32},{48,56},{56,48},{64,72... | collective-permute-start | bytes 393224 | tf_op jit(solution)/shard_map/ppermute | solution.py:141
  156.0 33.9 %collective-permute-start.27 = (bf16[512,128]{1,0:T(8,128)(2,1)S(1)}, bf16[512,128]{1,0:T(8,128)(2,1)S(1)}, u32[]{:S(2)}, u32[]{:S(2)}) collective-permute-start(bf16[512,128]{1,0:T(8,128)(2,1)S(1)} %get-tuple-element.226), channel_id=1, source_target_pairs={{0,56},{8,48},{16,40},{24,32},{32,24},{40,16},{48,8},{56,0},{64,12... | collective-permute-start | bytes 393224 | tf_op jit(solution)/shard_map/ppermute | solution.py:141
  185.4 11.9 %collective-permute-start.26 = (bf16[512,128]{1,0:T(8,128)(2,1)S(1)}, bf16[512,128]{1,0:T(8,128)(2,1)S(1)}, u32[]{:S(2)}, u32[]{:S(2)}) collective-permute-start(bf16[512,128]{1,0:T(8,128)(2,1)S(1)} %get-tuple-element.227), channel_id=1, source_target_pairs={{0,48},{8,56},{16,32},{24,40},{32,16},{40,24},{48,0},{56,8},{64,11... | collective-permute-start | bytes 393224 | tf_op jit(solution)/shard_map/ppermute | solution.py:141
  185.5 12.8 %collective-permute-start.25 = (bf16[512,128]{1,0:T(8,128)(2,1)S(1)}, bf16[512,128]{1,0:T(8,128)(2,1)S(1)}, u32[]{:S(2)}, u32[]{:S(2)}) collective-permute-start(bf16[512,128]{1,0:T(8,128)(2,1)S(1)} %get-tuple-element.228), channel_id=1, source_target_pairs={{0,40},{8,32},{16,56},{24,48},{32,8},{40,0},{48,24},{56,16},{64,10... | collective-permute-start | bytes 393224 | tf_op jit(solution)/shard_map/ppermute | solution.py:141
  185.5 18.1 %collective-permute-start.24 = (bf16[512,128]{1,0:T(8,128)(2,1)S(1)}, bf16[512,128]{1,0:T(8,128)(2,1)S(1)}, u32[]{:S(2)}, u32[]{:S(2)}) collective-permute-start(bf16[512,128]{1,0:T(8,128)(2,1)S(1)} %get-tuple-element.229), channel_id=1, source_target_pairs={{0,32},{8,40},{16,48},{24,56},{32,0},{40,8},{48,16},{56,24},{64,96... | collective-permute-start | bytes 393224 | tf_op jit(solution)/shard_map/ppermute | solution.py:141
  189.1 14.6 %collective-permute-start.23 = (bf16[512,128]{1,0:T(8,128)(2,1)S(1)}, bf16[512,128]{1,0:T(8,128)(2,1)S(1)}, u32[]{:S(2)}, u32[]{:S(2)}) collective-permute-start(bf16[512,128]{1,0:T(8,128)(2,1)S(1)} %get-tuple-element.230), channel_id=1, source_target_pairs={{0,24},{8,16},{16,8},{24,0},{32,56},{40,48},{48,40},{56,32},{64,88... | collective-permute-start | bytes 393224 | tf_op jit(solution)/shard_map/ppermute | solution.py:141
  190.0 13.7 %collective-permute-start.22 = (bf16[512,128]{1,0:T(8,128)(2,1)S(1)}, bf16[512,128]{1,0:T(8,128)(2,1)S(1)}, u32[]{:S(2)}, u32[]{:S(2)}) collective-permute-start(bf16[512,128]{1,0:T(8,128)(2,1)S(1)} %get-tuple-element.231), channel_id=1, source_target_pairs={{0,16},{8,24},{16,0},{24,8},{32,48},{40,56},{48,32},{56,40},{64,80... | collective-permute-start | bytes 393224 | tf_op jit(solution)/shard_map/ppermute | solution.py:141
  197.3 9.9 %collective-permute-start.14 = (bf16[512,128]{1,0:T(8,128)(2,1)S(1)}, bf16[512,128]{1,0:T(8,128)(2,1)S(1)}, u32[]{:S(2)}, u32[]{:S(2)}) collective-permute-start(bf16[512,128]{1,0:T(8,128)(2,1)S(1)} %get-tuple-element.232), channel_id=1, source_target_pairs={{0,8},{8,0},{16,24},{24,16},{32,40},{40,32},{48,56},{56,48},{64,72... | collective-permute-start | bytes 393224 | tf_op jit(solution)/shard_map/ppermute | solution.py:141
  198.3 9.5 %collective-permute-start.20 = (bf16[512,128]{1,0:T(8,128)(2,1)S(1)}, bf16[512,128]{1,0:T(8,128)(2,1)S(1)}, u32[]{:S(2)}, u32[]{:S(2)}) collective-permute-start(bf16[512,128]{1,0:T(8,128)(2,1)S(1)} %get-tuple-element.233), channel_id=1, source_target_pairs={{0,56},{8,48},{16,40},{24,32},{32,24},{40,16},{48,8},{56,0},{64,12... | collective-permute-start | bytes 393224 | tf_op jit(solution)/shard_map/ppermute | solution.py:141
  203.6 11.4 %collective-permute-start.19 = (bf16[512,128]{1,0:T(8,128)(2,1)S(1)}, bf16[512,128]{1,0:T(8,128)(2,1)S(1)}, u32[]{:S(2)}, u32[]{:S(2)}) collective-permute-start(bf16[512,128]{1,0:T(8,128)(2,1)S(1)} %get-tuple-element.234), channel_id=1, source_target_pairs={{0,48},{8,56},{16,32},{24,40},{32,16},{40,24},{48,0},{56,8},{64,11... | collective-permute-start | bytes 393224 | tf_op jit(solution)/shard_map/ppermute | solution.py:141
  203.7 11.3 %collective-permute-start.18 = (bf16[512,128]{1,0:T(8,128)(2,1)S(1)}, bf16[512,128]{1,0:T(8,128)(2,1)S(1)}, u32[]{:S(2)}, u32[]{:S(2)}) collective-permute-start(bf16[512,128]{1,0:T(8,128)(2,1)S(1)} %get-tuple-element.235), channel_id=1, source_target_pairs={{0,40},{8,32},{16,56},{24,48},{32,8},{40,0},{48,24},{56,16},{64,10... | collective-permute-start | bytes 393224 | tf_op jit(solution)/shard_map/ppermute | solution.py:141
  203.7 11.3 %collective-permute-start.17 = (bf16[512,128]{1,0:T(8,128)(2,1)S(1)}, bf16[512,128]{1,0:T(8,128)(2,1)S(1)}, u32[]{:S(2)}, u32[]{:S(2)}) collective-permute-start(bf16[512,128]{1,0:T(8,128)(2,1)S(1)} %get-tuple-element.236), channel_id=1, source_target_pairs={{0,32},{8,40},{16,48},{24,56},{32,0},{40,8},{48,16},{56,24},{64,96... | collective-permute-start | bytes 393224 | tf_op jit(solution)/shard_map/ppermute | solution.py:141
  207.2 9.7 %collective-permute-start.16 = (bf16[512,128]{1,0:T(8,128)(2,1)S(1)}, bf16[512,128]{1,0:T(8,128)(2,1)S(1)}, u32[]{:S(2)}, u32[]{:S(2)}) collective-permute-start(bf16[512,128]{1,0:T(8,128)(2,1)S(1)} %get-tuple-element.237), channel_id=1, source_target_pairs={{0,24},{8,16},{16,8},{24,0},{32,56},{40,48},{48,40},{56,32},{64,88... | collective-permute-start | bytes 393224 | tf_op jit(solution)/shard_map/ppermute | solution.py:141
  207.9 11.9 %collective-permute-start.15 = (bf16[512,128]{1,0:T(8,128)(2,1)S(1)}, bf16[512,128]{1,0:T(8,128)(2,1)S(1)}, u32[]{:S(2)}, u32[]{:S(2)}) collective-permute-start(bf16[512,128]{1,0:T(8,128)(2,1)S(1)} %get-tuple-element.238), channel_id=1, source_target_pairs={{0,16},{8,24},{16,0},{24,8},{32,48},{40,56},{48,32},{56,40},{64,80... | collective-permute-start | bytes 393224 | tf_op jit(solution)/shard_map/ppermute | solution.py:141
  (16 other events, 202.6 us)
